TPU v7x, 32 devices: a whole 2x2x4 slice. The times are simulated.
32 devices in a mesh: row: 8 (over z, core), col: 4 (over y, x).
Axes of the slice: x: 2, y: 2, z: 4, core: 2. Of those that a mesh axis runs over, the one named last changes fastest.
Arguments:
- activations: bfloat16 [1024, 8192], P('col', 'row'), may hold values from -6 to 6
- out_grad: bfloat16 [1024, 8192], P('col', 'row'), may hold values from -6 to 6
- gate_pre: bfloat16 [1024, 16384], P('row', 'col'), may hold values from -8 to 8
- up_proj: bfloat16 [1024, 16384], P('row', 'col'), may hold values from -6 to 6
- gate_weight: bfloat16 [8192, 16384], P('row', 'col'), may hold values from -0.0625 to 0.0625
- up_weight: bfloat16 [8192, 16384], P('row', 'col'), may hold values from -0.0625 to 0.0625
- down_weight: bfloat16 [16384, 8192], P('col', 'row'), may hold values from -0.046875 to 0.046875
Outputs:
- input_grad: bfloat16 [1024, 8192], P('col', 'row')
- gate_grad: bfloat16 [8192, 16384], P('row', 'col')
- up_grad: bfloat16 [8192, 16384], P('row', 'col')
- down_grad: bfloat16 [16384, 8192], P('col', 'row')
All inputs are finite; a program needn't handle non-finite values.
Results may differ from a plain program's by a relative error of at most 0.0051.
Values may be sent and summed in bfloat16 or wider, within the bound.
No kernel may reach another device: no remote copies, remote signals or barrier semaphores. Data moves between devices by JAX's collectives and lax.ppermute only.
A program may use at most 192 MiB of HBM per device.

v0:
```python
import jax
import jax.numpy as jnp
from jax import lax
from jax.sharding import PartitionSpec as P


def local_grads(gate_rows, up_rows, grad_rows):
    gate_float = gate_rows.astype(jnp.float32)
    up_float = up_rows.astype(jnp.float32)
    sigmoid_gate = jax.nn.sigmoid(gate_float)
    silu_gate = gate_float * sigmoid_gate
    hidden_act = (silu_gate * up_float).astype(jnp.bfloat16)
    gate_delta = (
        grad_rows * up_float * sigmoid_gate * (1.0 + gate_float * (1.0 - sigmoid_gate))
    ).astype(jnp.bfloat16)
    up_delta = (grad_rows * silu_gate).astype(jnp.bfloat16)
    return (hidden_act, gate_delta, up_delta)


def body(activations, out_grad, gate_pre, up_proj, gate_weight, up_weight, down_weight):
    act_full, grad_full = (
        lax.all_gather(activations, "col", axis=0, tiled=True),
        lax.all_gather(out_grad, "col", axis=0, tiled=True),
    )
    tokens_all = act_full.shape[0]
    contract_last = (((1,), (1,)), ((), ()))
    contract_first = (((0,), (0,)), ((), ()))
    grad_rows = grad_full
    hid_rows = lax.psum_scatter(
        lax.dot_general(grad_rows, down_weight, contract_last, preferred_element_type=jnp.float32),
        "row",
        scatter_dimension=0,
        tiled=True,
    )
    products = local_grads(gate_pre, up_proj, hid_rows)
    hidden_act = lax.all_gather(products[0], "row", axis=0, tiled=True)
    gate_delta = lax.all_gather(products[1], "row", axis=0, tiled=True)
    up_delta = lax.all_gather(products[2], "row", axis=0, tiled=True)
    grad_rows = grad_full
    acc_down = lax.dot_general(
        hidden_act, grad_rows, contract_first, preferred_element_type=jnp.float32
    )
    acc_gate = lax.dot_general(
        act_full, gate_delta, contract_first, preferred_element_type=jnp.float32
    )
    acc_up = lax.dot_general(act_full, up_delta, contract_first, preferred_element_type=jnp.float32)
    input_rows = lax.dot_general(
        gate_delta, gate_weight, contract_last, preferred_element_type=jnp.float32
    )
    input_rows = input_rows + lax.dot_general(
        up_delta, up_weight, contract_last, preferred_element_type=jnp.float32
    )
    acc_input = input_rows
    totals = (acc_down, acc_gate, acc_up, acc_input)
    acc_down, acc_gate, acc_up, acc_input = totals
    input_rows = lax.psum_scatter(acc_input, "col", scatter_dimension=0, tiled=True).astype(
        jnp.bfloat16
    )
    factor = float(tokens_all) ** (-0.5)
    return (
        input_rows,
        (acc_gate * factor).astype(jnp.bfloat16),
        (acc_up * factor).astype(jnp.bfloat16),
        (acc_down * factor).astype(jnp.bfloat16),
    )


def solution(mesh):
    in_specs = (
        P("col", "row"),
        P("col", "row"),
        P("row", "col"),
        P("row", "col"),
        P("row", "col"),
        P("row", "col"),
        P("col", "row"),
    )
    out_specs = (P("col", "row"), P("row", "col"), P("row", "col"), P("col", "row"))
    return jax.shard_map(body, mesh=mesh, in_specs=in_specs, out_specs=out_specs, check_vma=False)
```

profile of v0, /device:TPU:0, one launch (start us, length us, event | category | flops | bytes accessed | tf_op | source)
XLA Modules:
  0.0 582.2 jit_solution(11149804209979248327)
XLA Ops:
  7.2 0.0 all-gather.6.cloned.1.call-start
  7.2 0.7 all-gather.6.cloned.1.call-update
  7.9 0.0 reduce-scatter.3.cloned.1.call-start
  7.9 39.9 %all-gather.6.cloned.1.call-done = bf16[1024,1024]{1,0:T(8,128)(2,1)} async-done(((bf16[256,1024]{1,0:T(8,128)(2,1)}), bf16[1024,1024]{1,0:T(8,128)(2,1)}) %all-gather.6.cloned.1.call-update) | async-done | bytes 2097168 | tf_op jit(solution)/shard_map/all_gather | solution.py:23
  47.9 16.0 %fusion.10 = f32[1024,4096]{1,0:T(8,128)} fusion(bf16[1024,1024]{1,0:T(8,128)(2,1)} %all-gather.6.cloned.1.call-done, bf16[4096,1024]{1,0:T(8,128)(2,1)} %param.13), kind=kOutput, calls=%fused_computation.20 | convolution fusion | flops 8589934592 | bytes 27262976 | tf_op jit(solution)/shard_map/dot_general | solution.py:30
  63.9 0.0 copy-start
  63.9 0.0 copy-start.1
  63.9 0.0 reduce-scatter.3.cloned.1.call-update
  64.0 0.0 all-gather.8.cloned.1.call-start
  64.0 168.3 %reduce-scatter.3.cloned.1.call-done = f32[128,4096]{1,0:T(8,128)} async-done(((f32[1024,4096]{1,0:T(8,128)}), f32[128,4096]{1,0:T(8,128)}) %reduce-scatter.3.cloned.1.call-update) | async-done | bytes 2097168 | tf_op jit(solution)/shard_map/reduce_scatter | solution.py:29
  232.4 0.0 copy-done
  232.4 0.0 copy-done.1
  232.4 4.4 multiply_convert_fusion.3
  236.7 0.0 all-gather.8.cloned.1.call-update
  236.8 0.0 all-gather.10.cloned.1.call-start
  236.8 0.5 all-gather.10.cloned.1.call-update
  237.3 0.0 all-gather.12.cloned.1.call-start
  237.4 0.5 all-gather.12.cloned.1.call-update
  237.9 0.0 all-gather.14.cloned.1.call-start
  238.0 0.5 all-gather.14.cloned.1.call-update
  238.5 0.2 reduce-scatter.5.cloned.1.call-start
  238.7 78.6 %all-gather.8.cloned.1.call-done = bf16[1024,4096]{1,0:T(8,128)(2,1)} async-done(((bf16[128,4096]{1,0:T(8,128)(2,1)}), bf16[1024,4096]{1,0:T(8,128)(2,1)}) %all-gather.8.cloned.1.call-update) | async-done | bytes 8388624 | tf_op jit(solution)/shard_map/all_gather | solution.py:37
  317.3 15.0 %fusion.11 = f32[1024,1024]{1,0:T(8,128)} fusion(bf16[1024,4096]{1,0:T(8,128)(2,1)} %all-gather.8.cloned.1.call-done, bf16[1024,4096]{1,0:T(8,128)(2,1)} %param.11), kind=kOutput, calls=%fused_computation.21 | convolution fusion | flops 8589934592 | bytes 20971520 | tf_op jit(solution)/shard_map/dot_general | solution.py:47
  332.3 67.6 %all-gather.10.cloned.1.call-done = bf16[1024,4096]{1,0:T(8,128)(2,1)} async-done(((bf16[128,4096]{1,0:T(8,128)(2,1)}), bf16[1024,4096]{1,0:T(8,128)(2,1)}) %all-gather.10.cloned.1.call-update) | async-done | bytes 8388624 | tf_op jit(solution)/shard_map/all_gather | solution.py:38
  400.0 15.7 %convolution_add_fusion = f32[1024,1024]{1,0:T(8,128)} fusion(f32[1024,1024]{1,0:T(8,128)} %fusion.11, bf16[1024,4096]{1,0:T(8,128)(2,1)} %all-gather.10.cloned.1.call-done, bf16[1024,4096]{1,0:T(8,128)(2,1)} %param.12), kind=kOutput, calls=%fused_computation.19 | convolution fusion | flops 8590983168 | bytes 25165824 | tf_op jit(solution)/shard_map/dot_general | solution.py:50
  415.7 0.0 reduce-scatter.5.cloned.1.call-update
  415.7 19.8 %all-gather.12.cloned.1.call-done = bf16[1024,1024]{1,0:T(8,128)(2,1)} async-done(((bf16[256,1024]{1,0:T(8,128)(2,1)}), bf16[1024,1024]{1,0:T(8,128)(2,1)}) %all-gather.12.cloned.1.call-update) | async-done | bytes 2097168 | tf_op jit(solution)/shard_map/all_gather | solution.py:22
  435.5 14.9 %fusion = bf16[1024,4096]{0,1:T(8,128)(2,1)} fusion(bf16[1024,4096]{1,0:T(8,128)(2,1)} %all-gather.8.cloned.1.call-done, bf16[1024,1024]{1,0:T(8,128)(2,1)} %all-gather.12.cloned.1.call-done), kind=kOutput, calls=%fused_computation.3 | convolution fusion | flops 8598323200 | bytes 18874368 | tf_op jit(solution)/shard_map/dot_general | solution.py:43
  450.4 0.0 copy-start.3
  450.4 12.1 %copy.11 = bf16[1024,4096]{1,0:T(8,128)(2,1)} copy(bf16[1024,4096]{0,1:T(8,128)(2,1)} %fusion) | data formatting | bytes 16777216
  462.5 0.0 copy-done.3
  462.5 14.7 %fusion.1 = bf16[1024,4096]{0,1:T(8,128)(2,1)} fusion(bf16[1024,4096]{1,0:T(8,128)(2,1)} %all-gather.10.cloned.1.call-done, bf16[1024,1024]{1,0:T(8,128)(2,1)S(1)} %copy-done.3), kind=kOutput, calls=%fused_computation.4 | convolution fusion | flops 8598323200 | bytes 18874368 | tf_op jit(solution)/shard_map/dot_general | solution.py:46
  477.2 0.0 copy-start.2
  477.2 12.1 %copy.12 = bf16[1024,4096]{1,0:T(8,128)(2,1)} copy(bf16[1024,4096]{0,1:T(8,128)(2,1)} %fusion.1) | data formatting | bytes 16777216
  489.3 29.8 %all-gather.14.cloned.1.call-done = bf16[1024,4096]{1,0:T(8,128)(2,1)} async-done(((bf16[128,4096]{1,0:T(8,128)(2,1)}), bf16[1024,4096]{1,0:T(8,128)(2,1)}) %all-gather.14.cloned.1.call-update) | async-done | bytes 8388624 | tf_op jit(solution)/shard_map/all_gather | solution.py:36
  519.1 0.0 copy-done.2
  519.1 14.6 %multiply_convert_fusion = bf16[4096,1024]{1,0:T(8,128)(2,1)} fusion(bf16[1024,4096]{1,0:T(8,128)(2,1)} %all-gather.14.cloned.1.call-done, bf16[1024,1024]{1,0:T(8,128)(2,1)S(1)} %copy-done.2), kind=kOutput, calls=%fused_computation | convolution fusion | flops 8598323200 | bytes 18874368 | tf_op jit(solution)/shard_map/dot_general | solution.py:40
  533.6 39.7 %reduce-scatter.5.cloned.1.call-done = f32[256,1024]{1,0:T(8,128)} async-done(((f32[1024,1024]{1,0:T(8,128)}), f32[256,1024]{1,0:T(8,128)}) %reduce-scatter.5.cloned.1.call-update) | async-done | bytes 1048592 | tf_op jit(solution)/shard_map/reduce_scatter | solution.py:56
  573.3 2.1 convert_element_type.37
Async XLA Ops:
  7.2 40.7 %all-gather.6.cloned.1.call-start = ((), (), s32[]{:S(2)}) async-start(), calls=%async_computation.2 | async-start | bytes 2621440 | tf_op jit(solution)/shard_map/all_gather | solution.py:23
  7.9 224.5 %reduce-scatter.3.cloned.1.call-start = ((), (), s32[]{:S(2)}) async-start(), calls=%async_computation.3 | async-start | bytes 18874368 | tf_op jit(solution)/shard_map/reduce_scatter | solution.py:29
  63.9 168.4 %copy-start = (bf16[128,4096]{1,0:T(8,128)(2,1)S(1)}, bf16[128,4096]{1,0:T(8,128)(2,1)}, u32[]{:S(2)}) copy-start(bf16[128,4096]{1,0:T(8,128)(2,1)} %param.9) | copy-start | bytes 3145732
  63.9 168.4 %copy-start.1 = (bf16[128,4096]{1,0:T(8,128)(2,1)S(1)}, bf16[128,4096]{1,0:T(8,128)(2,1)}, u32[]{:S(2)}) copy-start(bf16[128,4096]{1,0:T(8,128)(2,1)} %param.10) | copy-start | bytes 3145732
  64.0 253.3 %all-gather.8.cloned.1.call-start = ((), (), s32[]{:S(2)}) async-start(), calls=%async_computation.4 | async-start | bytes 9437184 | tf_op jit(solution)/shard_map/all_gather | solution.py:37
  236.8 163.2 %all-gather.10.cloned.1.call-start = ((), (), s32[]{:S(2)}) async-start(), calls=%async_computation.5 | async-start | bytes 9437184 | tf_op jit(solution)/shard_map/all_gather | solution.py:38
  237.3 198.2 %all-gather.12.cloned.1.call-start = ((), (), s32[]{:S(2)}) async-start(), calls=%async_computation.7 | async-start | bytes 2621440 | tf_op jit(solution)/shard_map/all_gather | solution.py:22
  237.9 281.1 %all-gather.14.cloned.1.call-start = ((), (), s32[]{:S(2)}) async-start(), calls=%async_computation.8 | async-start | bytes 9437184 | tf_op jit(solution)/shard_map/all_gather | solution.py:36
  238.5 334.8 %reduce-scatter.5.cloned.1.call-start = ((), (), s32[]{:S(2)}) async-start(), calls=%async_computation.6 | async-start | bytes 5242880 | tf_op jit(solution)/shard_map/reduce_scatter | solution.py:56
  450.4 12.1 %copy-start.3 = (bf16[1024,1024]{1,0:T(8,128)(2,1)S(1)}, bf16[1024,1024]{1,0:T(8,128)(2,1)}, u32[]{:S(2)}) copy-start(bf16[1024,1024]{1,0:T(8,128)(2,1)} %all-gather.12.cloned.1.call-done) | copy-start | bytes 6291460
  477.2 41.9 %copy-start.2 = (bf16[1024,1024]{1,0:T(8,128)(2,1)S(1)}, bf16[1024,1024]{1,0:T(8,128)(2,1)}, u32[]{:S(2)}) copy-start(bf16[1024,1024]{1,0:T(8,128)(2,1)} %all-gather.6.cloned.1.call-done) | copy-start | bytes 6291460
Sparse Core Ops, SparseCore 0:
  9.8 38.0 all-gather.5
  64.1 168.2 reduce-scatter.2
  236.9 80.3 all-gather.7
  319.3 80.5 all-gather.9
  401.6 33.8 all-gather.11
  437.0 82.0 all-gather.13
  522.0 51.2 reduce-scatter.4
where the time goes:
time: 583 us; the launch traced here: 582 us
  waiting for transfers between devices  446 us (77%)
  matrix products  90.9 us (16%)
  local copies, waits for them, and re-layouts  24.2 us (4%)
  between operations  14.1 us (2%)
  other arithmetic  6.46 us (1%)
    reduce_scatter x1, waiting for transfers between devices, body(): lax.psum_scatter(lax.dot_general(grad_rows, down_weight, contract_last, p...  168 us
    all_gather x1, waiting for transfers between devices, body(): gate_delta = lax.all_gather(products[1], 'row', axis=0, tiled=True)  78.6 us
    all_gather x1, waiting for transfers between devices, body(): up_delta = lax.all_gather(products[2], 'row', axis=0, tiled=True)  67.6 us
    all_gather x1, waiting for transfers between devices, body(): lax.all_gather(out_grad, 'col', axis=0, tiled=True)  39.9 us
    reduce_scatter x1, waiting for transfers between devices, body(): lax.psum_scatter(acc_input, 'col', scatter_dimension=0, tiled=True)  39.7 us
    all_gather x1, waiting for transfers between devices, body(): hidden_act = lax.all_gather(products[0], 'row', axis=0, tiled=True)  29.8 us
    unnamed x10, local copies, waits for them, and re-layouts  24.2 us
    all_gather x1, waiting for transfers between devices, body(): lax.all_gather(activations, 'col', axis=0, tiled=True)  19.8 us
  transfers between devices with their start and end apart: 7, of which 7 were waited for; matrix products, arithmetic and copies ran while one was open for 17% of the time, Pallas kernels for 0%

commit v1 on v0

--- a/solution.py
+++ b/solution.py
@@ -2,6 +2,16 @@
 import jax.numpy as jnp
 from jax import lax
 from jax.sharding import PartitionSpec as P
+
+
+def gather_by_hops(x, name, along):
+    count = lax.axis_size(name)
+    moving, parts = (x, [x])
+    for _ in range(count - 1):
+        moving = lax.ppermute(moving, name, [(i, (i + 1) % count) for i in range(count)])
+        parts.insert(0, moving)
+    row_of_blocks = jnp.concatenate(parts, axis=along)
+    return jnp.roll(row_of_blocks, (lax.axis_index(name) + 1) * x.shape[along], axis=along)
 
 
 def local_grads(gate_rows, up_rows, grad_rows):
@@ -35,7 +45,7 @@
     products = local_grads(gate_pre, up_proj, hid_rows)
     hidden_act = lax.all_gather(products[0], "row", axis=0, tiled=True)
     gate_delta = lax.all_gather(products[1], "row", axis=0, tiled=True)
-    up_delta = lax.all_gather(products[2], "row", axis=0, tiled=True)
+    up_delta = gather_by_hops(products[2], "row", 0)
     grad_rows = grad_full
     acc_down = lax.dot_general(
         hidden_act, grad_rows, contract_first, preferred_element_type=jnp.float32

time: 583 us -> 561 us (0.962)
  waiting for transfers between devices: 446 us -> 399 us
  local copies, waits for them, and re-layouts: 24.2 us -> 52.5 us
    ppermute x0 -> x7, waiting for transfers between devices: none -> 190 us  [gather_by_hops(): lax.ppermute(moving, name, [(i, (i + 1) % count) for i in range(count)])]
    all_gather x1, waiting for transfers between devices: 78.6 us -> 0.01 us  [body(): gate_delta = lax.all_gather(products[1], 'row', axis=0, tiled=True)]
    all_gather x1 -> x0, waiting for transfers between devices: 67.6 us -> none  [body(): up_delta = lax.all_gather(products[2], 'row', axis=0, tiled=True)]
    reduce_scatter x1, waiting for transfers between devices: 39.7 us -> 0.01 us  [body(): lax.psum_scatter(acc_input, 'col', scatter_dimension=0, tiled=True)]
    all_gather x1, waiting for transfers between devices: 29.8 us -> 0.01 us  [body(): hidden_act = lax.all_gather(products[0], 'row', axis=0, tiled=True)]
    unnamed x10 -> x29, local copies, waits for them, and re-layouts: 24.2 us -> 51.5 us
    all_gather x1, waiting for transfers between devices: 19.8 us -> 0.02 us  [body(): lax.all_gather(activations, 'col', axis=0, tiled=True)]
  transfers between devices with their start and end apart: 7 -> 13, of which waited for: 7 -> 9; matrix products, arithmetic and copies ran while one was open for 17% -> 22% of each run, Pallas kernels for 0% -> 0%
where the time goes in v1:
time: 561 us; the launch traced here: 560 us
  waiting for transfers between devices  399 us (71%)
  matrix products  88 us (16%)
  local copies, waits for them, and re-layouts  52.5 us (9%)
  between operations  14.2 us (3%)
  other arithmetic  6.23 us (1%)
    ppermute x7, waiting for transfers between devices, gather_by_hops(): lax.ppermute(moving, name, [(i, (i + 1) % count) for i in range(count)])  190 us
    reduce_scatter x1, waiting for transfers between devices, body(): lax.psum_scatter(lax.dot_general(grad_rows, down_weight, contract_last, p...  168 us
    unnamed x29, local copies, waits for them, and re-layouts  51.5 us
    all_gather x1, waiting for transfers between devices, body(): lax.all_gather(out_grad, 'col', axis=0, tiled=True)  39.9 us
    dot_general x1, matrix products, body(): lax.dot_general(grad_rows, down_weight, contract_last, preferred_element_...  16 us
    dot_general x1, matrix products, body(): lax.dot_general(up_delta, up_weight, contract_last, preferred_element_typ...  15.2 us
    dot_general x1, matrix products, body(): lax.dot_general(act_full, up_delta, contract_first, preferred_element_typ...  14.9 us
    dot_general x1, matrix products, body(): lax.dot_general(act_full, gate_delta, contract_first, preferred_element_t...  14.7 us
  transfers between devices with their start and end apart: 13, of which 9 were waited for; matrix products, arithmetic and copies ran while one was open for 22% of the time, Pallas kernels for 0%

profile of v1, /device:TPU:0, one launch (start us, length us, event | category | flops | bytes accessed | tf_op | source)
XLA Modules:
  0.0 560.4 jit_solution(3883867988134683051)
XLA Ops:
  7.2 0.0 all-gather.5.cloned.1.call-start
  7.2 0.7 all-gather.5.cloned.1.call-update
  7.9 0.0 reduce-scatter.3.cloned.1.call-start
  7.9 39.9 %all-gather.5.cloned.1.call-done = bf16[1024,1024]{1,0:T(8,128)(2,1)} async-done(((bf16[256,1024]{1,0:T(8,128)(2,1)}), bf16[1024,1024]{1,0:T(8,128)(2,1)}) %all-gather.5.cloned.1.call-update) | async-done | bytes 2097168 | tf_op jit(solution)/shard_map/all_gather | solution.py:33
  47.9 16.0 %fusion.20 = f32[1024,4096]{1,0:T(8,128)} fusion(bf16[1024,1024]{1,0:T(8,128)(2,1)} %all-gather.5.cloned.1.call-done, bf16[4096,1024]{1,0:T(8,128)(2,1)} %param.13), kind=kOutput, calls=%fused_computation.41 | convolution fusion | flops 8589934592 | bytes 27262976 | tf_op jit(solution)/shard_map/dot_general | solution.py:40
  64.0 0.0 all-gather.7.cloned.1.call-start
  64.0 168.3 %reduce-scatter.3.cloned.1.call-done = f32[128,4096]{1,0:T(8,128)} async-done(((f32[1024,4096]{1,0:T(8,128)}), f32[128,4096]{1,0:T(8,128)}) %reduce-scatter.3.cloned.1.call-update) | async-done | bytes 2097168 | tf_op jit(solution)/shard_map/reduce_scatter | solution.py:39
  232.4 4.1 multiply_convert_fusion.3
  236.5 0.0 all-gather.7.cloned.1.call-update
  236.5 0.0 all-gather.9.cloned.1.call-start
  236.6 0.1 collective-permute-start
  236.6 25.6 %collective-permute-done = bf16[128,4096]{1,0:T(8,128)(2,1)S(1)} collective-permute-done((bf16[128,4096]{1,0:T(8,128)(2,1)S(1)}, bf16[128,4096]{1,0:T(8,128)(2,1)S(1)}, u32[]{:S(2)}, u32[]{:S(2)}) %collective-permute-start) | collective-permute-done | bytes 1048608 | tf_op jit(solution)/shard_map/ppermute | solution.py:11
  262.2 0.0 all-gather.9.cloned.1.call-update
  262.3 0.0 all-gather.11.cloned.1.call-start
  262.3 38.4 %collective-permute-done.1 = bf16[128,4096]{1,0:T(8,128)(2,1)S(1)} collective-permute-done((bf16[128,4096]{1,0:T(8,128)(2,1)S(1)}, bf16[128,4096]{1,0:T(8,128)(2,1)S(1)}, u32[]{:S(2)}, u32[]{:S(2)}) %collective-permute-start.1) | collective-permute-done | bytes 1048608 | tf_op jit(solution)/shard_map/ppermute | solution.py:11
  300.7 38.5 %collective-permute-done.2 = bf16[128,4096]{1,0:T(8,128)(2,1)S(1)} collective-permute-done((bf16[128,4096]{1,0:T(8,128)(2,1)S(1)}, bf16[128,4096]{1,0:T(8,128)(2,1)S(1)}, u32[]{:S(2)}, u32[]{:S(2)}) %collective-permute-start.2) | collective-permute-done | bytes 1048608 | tf_op jit(solution)/shard_map/ppermute | solution.py:11
  339.2 1.0 copy-done
  340.2 16.1 %collective-permute-done.3 = bf16[128,4096]{1,0:T(8,128)(2,1)} collective-permute-done((bf16[128,4096]{1,0:T(8,128)(2,1)S(1)}, bf16[128,4096]{1,0:T(8,128)(2,1)}, u32[]{:S(2)}, u32[]{:S(2)}) %collective-permute-start.3) | collective-permute-done | bytes 1048608 | tf_op jit(solution)/shard_map/ppermute | solution.py:11
  356.3 0.0 all-gather.11.cloned.1.call-update
  356.3 0.0 reduce-scatter.5.cloned.1.call-start
  356.4 16.3 %collective-permute-done.4 = bf16[128,4096]{1,0:T(8,128)(2,1)} collective-permute-done((bf16[128,4096]{1,0:T(8,128)(2,1)}, bf16[128,4096]{1,0:T(8,128)(2,1)}, u32[]{:S(2)}, u32[]{:S(2)}) %collective-permute-start.4) | collective-permute-done | bytes 1048608 | tf_op jit(solution)/shard_map/ppermute | solution.py:11
  372.6 16.3 %collective-permute-done.5 = bf16[128,4096]{1,0:T(8,128)(2,1)} collective-permute-done((bf16[128,4096]{1,0:T(8,128)(2,1)}, bf16[128,4096]{1,0:T(8,128)(2,1)}, u32[]{:S(2)}, u32[]{:S(2)}) %collective-permute-start.5) | collective-permute-done | bytes 1048608 | tf_op jit(solution)/shard_map/ppermute | solution.py:11
  389.0 38.8 %collective-permute-done.6 = bf16[128,4096]{1,0:T(8,128)(2,1)} collective-permute-done((bf16[128,4096]{1,0:T(8,128)(2,1)}, bf16[128,4096]{1,0:T(8,128)(2,1)}, u32[]{:S(2)}, u32[]{:S(2)}) %collective-permute-start.6) | collective-permute-done | bytes 1048608 | tf_op jit(solution)/shard_map/ppermute | solution.py:11
  427.8 2.4 constant_dynamic-update-slice_fusion.15
  430.2 2.3 constant_dynamic-update-slice_fusion.14
  432.4 2.3 constant_dynamic-update-slice_fusion.13
  434.7 2.3 constant_dynamic-update-slice_fusion.12
  437.0 1.1 constant_dynamic-update-slice_fusion.11
  438.1 1.1 constant_dynamic-update-slice_fusion.10
  439.2 1.0 constant_dynamic-update-slice_fusion.9
  440.2 1.2 constant_dynamic-update-slice_fusion.8
  441.4 2.4 constant_dynamic-update-slice_fusion.7
  443.8 2.3 constant_dynamic-update-slice_fusion.6
  446.1 2.3 constant_dynamic-update-slice_fusion.5
  448.4 2.3 constant_dynamic-update-slice_fusion.4
  450.7 1.1 constant_dynamic-update-slice_fusion.3
  451.8 1.1 constant_dynamic-update-slice_fusion.2
  452.9 1.1 constant_dynamic-update-slice_fusion.1
  453.9 1.1 constant_dynamic-update-slice_fusion
  455.0 12.7 %fusion.21 = f32[1024,1024]{1,0:T(8,128)S(1)} fusion(bf16[1024,4096]{1,0:T(8,128)(2,1)} %all-gather.7.cloned.1.call-done, bf16[1024,4096]{1,0:T(8,128)(2,1)} %param.11), kind=kOutput, calls=%fused_computation.42 | convolution fusion | flops 8589934592 | bytes 20971520 | tf_op jit(solution)/shard_map/dot_general | solution.py:57
  467.7 15.2 %fusion.15 = f32[1024,1024]{1,0:T(8,128)} fusion(f32[1024,1024]{1,0:T(8,128)S(1)} %fusion.21, bf16[1024,4096]{1,0:T(8,128)(2,1)} %param.12, bf16[2048,4096]{1,0:T(8,128)(2,1)} %constant_dynamic-update-slice_fusion, s32[]{:T(128)S(6)} %select_n.14), kind=kOutput, calls=%fused_computation.22 | convolution fusion | flops 8590983168 | bytes 25165828 | tf_op jit(solution)/shard_map/dot_general | solution.py:60
  482.9 0.0 all-gather.9.cloned.1.call-done
  482.9 14.9 %fusion.4 = bf16[1024,4096]{0,1:T(8,128)(2,1)} fusion(bf16[1024,1024]{1,0:T(8,128)(2,1)} %all-gather.9.cloned.1.call-done, bf16[2048,4096]{1,0:T(8,128)(2,1)} %constant_dynamic-update-slice_fusion, s32[]{:T(128)S(6)} %select_n.14), kind=kOutput, calls=%fused_computation.7 | convolution fusion | flops 8598323200 | bytes 18874372 | tf_op jit(solution)/shard_map/dot_general | solution.py:56
  497.9 12.2 %copy.12 = bf16[1024,4096]{1,0:T(8,128)(2,1)} copy(bf16[1024,4096]{0,1:T(8,128)(2,1)} %fusion.4) | data formatting | bytes 16777216
  510.0 14.7 %fusion.3 = bf16[1024,4096]{0,1:T(8,128)(2,1)} fusion(bf16[1024,4096]{1,0:T(8,128)(2,1)} %all-gather.7.cloned.1.call-done, bf16[1024,1024]{1,0:T(8,128)(2,1)S(1)} %copy-done.5), kind=kOutput, calls=%fused_computation.6 | convolution fusion | flops 8598323200 | bytes 18874368 | tf_op jit(solution)/shard_map/dot_general | solution.py:53
  524.7 12.1 %copy.11 = bf16[1024,4096]{1,0:T(8,128)(2,1)} copy(bf16[1024,4096]{0,1:T(8,128)(2,1)} %fusion.3) | data formatting | bytes 16777216
  536.8 14.6 %multiply_convert_fusion = bf16[4096,1024]{1,0:T(8,128)(2,1)} fusion(bf16[1024,4096]{1,0:T(8,128)(2,1)} %all-gather.11.cloned.1.call-done, bf16[1024,1024]{1,0:T(8,128)(2,1)S(1)} %copy-done.4), kind=kOutput, calls=%fused_computation | convolution fusion | flops 8598323200 | bytes 18874368 | tf_op jit(solution)/shard_map/dot_general | solution.py:50
  551.4 2.1 convert_element_type.37
  (22 shorter events, 0.1 us)
Async XLA Ops:
  7.2 40.7 %all-gather.5.cloned.1.call-start = ((), (), s32[]{:S(2)}) async-start(), calls=%async_computation.2 | async-start | bytes 2621440 | tf_op jit(solution)/shard_map/all_gather | solution.py:33
  7.9 224.5 %reduce-scatter.3.cloned.1.call-start = ((), (), s32[]{:S(2)}) async-start(), calls=%async_computation.3 | async-start | bytes 18874368 | tf_op jit(solution)/shard_map/reduce_scatter | solution.py:39
  63.9 168.4 %copy-start.2 = (bf16[128,4096]{1,0:T(8,128)(2,1)S(1)}, bf16[128,4096]{1,0:T(8,128)(2,1)}, u32[]{:S(2)}) copy-start(bf16[128,4096]{1,0:T(8,128)(2,1)} %param.9) | copy-start | bytes 3145732
  63.9 168.4 %copy-start.3 = (bf16[128,4096]{1,0:T(8,128)(2,1)S(1)}, bf16[128,4096]{1,0:T(8,128)(2,1)}, u32[]{:S(2)}) copy-start(bf16[128,4096]{1,0:T(8,128)(2,1)} %param.10) | copy-start | bytes 3145732
  64.0 391.1 %all-gather.7.cloned.1.call-start = ((), (), s32[]{:S(2)}) async-start(), calls=%async_computation.4 | async-start | bytes 9437184 | tf_op jit(solution)/shard_map/all_gather | solution.py:47
  236.5 246.4 %all-gather.9.cloned.1.call-start = ((), (), s32[]{:S(2)}) async-start(), calls=%async_computation.6 | async-start | bytes 2621440 | tf_op jit(solution)/shard_map/all_gather | solution.py:32
  236.6 25.7 %collective-permute-start = (bf16[128,4096]{1,0:T(8,128)(2,1)S(1)}, bf16[128,4096]{1,0:T(8,128)(2,1)S(1)}, u32[]{:S(2)}, u32[]{:S(2)}) collective-permute-start(bf16[128,4096]{1,0:T(8,128)(2,1)S(1)} %get-tuple-element.8), channel_id=1, source_target_pairs={{0,4},{4,8},{8,12},{12,16},{16,20},{20,24},{24,28},{28,0},{1,5},{5... | collective-permute-start | bytes 3145736 | tf_op jit(solution)/shard_map/ppermute | solution.py:11
  262.2 38.5 %collective-permute-start.1 = (bf16[128,4096]{1,0:T(8,128)(2,1)S(1)}, bf16[128,4096]{1,0:T(8,128)(2,1)S(1)}, u32[]{:S(2)}, u32[]{:S(2)}) collective-permute-start(bf16[128,4096]{1,0:T(8,128)(2,1)S(1)} %collective-permute-done), channel_id=1, source_target_pairs={{0,4},{4,8},{8,12},{12,16},{16,20},{20,24},{24,28},{28,0},{1,5},{5... | collective-permute-start | bytes 3145736 | tf_op jit(solution)/shard_map/ppermute | solution.py:11
  262.3 274.6 %all-gather.11.cloned.1.call-start = ((), (), s32[]{:S(2)}) async-start(), calls=%async_computation.7 | async-start | bytes 9437184 | tf_op jit(solution)/shard_map/all_gather | solution.py:46
  300.7 38.5 %collective-permute-start.2 = (bf16[128,4096]{1,0:T(8,128)(2,1)S(1)}, bf16[128,4096]{1,0:T(8,128)(2,1)S(1)}, u32[]{:S(2)}, u32[]{:S(2)}) collective-permute-start(bf16[128,4096]{1,0:T(8,128)(2,1)S(1)} %collective-permute-done.1), channel_id=1, source_target_pairs={{0,4},{4,8},{8,12},{12,16},{16,20},{20,24},{24,28},{28,0},{1,5},{5... | collective-permute-start | bytes 3145736 | tf_op jit(solution)/shard_map/ppermute | solution.py:11
  339.2 1.0 copy-start
  340.2 16.1 %collective-permute-start.3 = (bf16[128,4096]{1,0:T(8,128)(2,1)S(1)}, bf16[128,4096]{1,0:T(8,128)(2,1)}, u32[]{:S(2)}, u32[]{:S(2)}) collective-permute-start(bf16[128,4096]{1,0:T(8,128)(2,1)S(1)} %collective-permute-done.2), channel_id=1, source_target_pairs={{0,4},{4,8},{8,12},{12,16},{16,20},{20,24},{24,28},{28,0},{1,5},{5... | collective-permute-start | bytes 3145736 | tf_op jit(solution)/shard_map/ppermute | solution.py:11
  356.3 16.3 %collective-permute-start.4 = (bf16[128,4096]{1,0:T(8,128)(2,1)}, bf16[128,4096]{1,0:T(8,128)(2,1)}, u32[]{:S(2)}, u32[]{:S(2)}) collective-permute-start(bf16[128,4096]{1,0:T(8,128)(2,1)} %collective-permute-done.3), channel_id=1, source_target_pairs={{0,4},{4,8},{8,12},{12,16},{16,20},{20,24},{24,28},{28,0},{1,5},{5... | collective-permute-start | bytes 3145736 | tf_op jit(solution)/shard_map/ppermute | solution.py:11
  356.3 195.1 %reduce-scatter.5.cloned.1.call-start = ((), (), s32[]{:S(2)}) async-start(), calls=%async_computation.5 | async-start | bytes 5242880 | tf_op jit(solution)/shard_map/reduce_scatter | solution.py:66
  372.6 16.3 %collective-permute-start.5 = (bf16[128,4096]{1,0:T(8,128)(2,1)}, bf16[128,4096]{1,0:T(8,128)(2,1)}, u32[]{:S(2)}, u32[]{:S(2)}) collective-permute-start(bf16[128,4096]{1,0:T(8,128)(2,1)} %collective-permute-done.4), channel_id=1, source_target_pairs={{0,4},{4,8},{8,12},{12,16},{16,20},{20,24},{24,28},{28,0},{1,5},{5... | collective-permute-start | bytes 3145736 | tf_op jit(solution)/shard_map/ppermute | solution.py:11
  389.0 38.8 %collective-permute-start.6 = (bf16[128,4096]{1,0:T(8,128)(2,1)}, bf16[128,4096]{1,0:T(8,128)(2,1)}, u32[]{:S(2)}, u32[]{:S(2)}) collective-permute-start(bf16[128,4096]{1,0:T(8,128)(2,1)} %collective-permute-done.5), channel_id=1, source_target_pairs={{0,4},{4,8},{8,12},{12,16},{16,20},{20,24},{24,28},{28,0},{1,5},{5... | collective-permute-start | bytes 3145736 | tf_op jit(solution)/shard_map/ppermute | solution.py:11
  389.0 48.1 %copy-start.1 = (bf16[128,4096]{1,0:T(8,128)(2,1)S(1)}, bf16[128,4096]{1,0:T(8,128)(2,1)}, u32[]{:S(2)}) copy-start(bf16[128,4096]{1,0:T(8,128)(2,1)} %copy-done) | copy-start | bytes 3145732
  497.9 12.2 %copy-start.5 = (bf16[1024,1024]{1,0:T(8,128)(2,1)S(1)}, bf16[1024,1024]{1,0:T(8,128)(2,1)}, u32[]{:S(2)}) copy-start(bf16[1024,1024]{1,0:T(8,128)(2,1)} %all-gather.9.cloned.1.call-done) | copy-start | bytes 6291460
  524.7 12.1 %copy-start.4 = (bf16[1024,1024]{1,0:T(8,128)(2,1)S(1)}, bf16[1024,1024]{1,0:T(8,128)(2,1)}, u32[]{:S(2)}) copy-start(bf16[1024,1024]{1,0:T(8,128)(2,1)} %all-gather.5.cloned.1.call-done) | copy-start | bytes 6291460
Sparse Core Ops, SparseCore 0:
  9.8 38.0 all-gather.4
  64.1 168.2 reduce-scatter.2
  236.6 107.5 all-gather.6
  346.0 33.5 all-gather.8
  381.0 93.1 all-gather.10
  483.0 50.8 reduce-scatter.4
